TPU v7x, 256 devices: a whole 4x4x8 slice. The times are simulated.
256 devices in a mesh: dp: 16 (over z_lo, y, core), ctx: 16 (over x, z_hi).
Axes of the slice: x: 4, y: 4, z: 8 (z_hi: 4, z_lo: 2; z = z_hi * 2 + z_lo), core: 2. Of those that a mesh axis runs over, the one named last changes fastest.
Arguments:
- tokens: bfloat16 [16, 2048, 2560], P('dp', 'ctx'), may hold values from -6 to 6
- shard_counts: int32 [16, 16], P('dp'), may hold values from 64 to 128, as said below
- stretch_start: int32 [16], P('dp'), may hold values from 102 to 409, as said below
- segment_ids: int32 [16, 2048], P('dp', 'ctx'), may hold values from 0 to 1, as said below
- span_ids: int32 [16, 2048], P('dp', 'ctx'), may hold values from -1 to 31, as said below
- query_weight: bfloat16 [2560, 2560], P('dp'), may hold values from -0.125 to 0.125
- key_matrix: bfloat16 [2560, 512], P('dp'), may hold values from -0.125 to 0.125
- value_matrix: bfloat16 [2560, 512], P('dp'), may hold values from -0.125 to 0.125
- score_vector: bfloat16 [2560], replicated, may hold values from -4 to 4
Outputs:
- attention: bfloat16 [16, 2048, 2560], P('dp', 'ctx')
- candidate_loglik: float32 [16, 32], P('dp')
Inputs may be any that keep to these rules, and one draw needn't show every extreme that they name: `shard_counts`: in every sequence at least one shard has exactly 128 live tokens. `stretch_start`: A stretch of each sequence starts at a position held by one of its live tokens, after the first. `segment_ids`: along the live tokens of a sequence, segment ids never fall. `span_ids`: each candidate of every sequence covers one or more live tokens, in one run of consecutive positions; empty slots have -1.
All inputs are finite; a program needn't handle non-finite values.
Results may differ from a plain program's by a relative error of at most 0.0066.
Values may be sent and summed in bfloat16 or wider, within the bound.
No kernel may reach another device: no remote copies, remote signals or barrier semaphores. Data moves between devices by JAX's collectives and lax.ppermute only.
A program may use at most 128 MiB of HBM per device.

v0:
```python
import math
import jax
import jax.numpy as jnp
from jax import lax
from jax.sharding import PartitionSpec as P

QUERY_HEADS = 20
KEY_VALUE_HEADS = 4
HEAD_SIZE = 128
STRETCH = 8192
CAND = 32
THETA = 500000.0
EPS = 1e-05


def rotary_then_norm(value_rows, token_places, heads):
    token_count = value_rows.shape[0]
    half = HEAD_SIZE // 2
    shaped = value_rows.reshape(token_count, heads, HEAD_SIZE)
    freqs = jnp.exp(jnp.arange(half, dtype=jnp.float32) * (-2.0 * math.log(THETA) / HEAD_SIZE))
    angles = token_places.astype(jnp.float32)[:, None] * freqs[None, :]
    cosine = jnp.cos(angles)[:, None, :]
    sine = jnp.sin(angles)[:, None, :]
    leading_block = shaped[..., :half]
    second = shaped[..., half:]
    turned = jnp.concatenate(
        [leading_block * cosine - second * sine, second * cosine + leading_block * sine], axis=-1
    )
    scale = lax.rsqrt(jnp.mean(turned * turned, axis=-1, keepdims=True) + EPS)
    return (turned * scale).astype(jnp.bfloat16).reshape(token_count, heads * HEAD_SIZE)


def per_device(
    tokens,
    shard_counts,
    stretch_start,
    segment_ids,
    span_ids,
    query_weight,
    key_matrix,
    value_matrix,
    score_vector,
):
    inputs = tokens[0]
    token_slots = inputs.shape[0]
    shards = lax.axis_size("ctx")
    mine = lax.axis_index("ctx")
    counts = shard_counts[0]
    order = jnp.arange(shards, dtype=jnp.int32)
    count_mine = jnp.sum(jnp.where(order == mine, counts, 0))
    start_mine = jnp.sum(jnp.where(order < mine, counts, 0))
    offsets = jnp.arange(token_slots, dtype=jnp.int32)
    token_places = start_mine + offsets
    live = offsets < count_mine
    cstart = stretch_start[0]
    qseg = segment_ids[0]
    qchunk = (token_places + STRETCH - cstart) // STRETCH
    pieces = (
        lax.all_gather(query_weight, "dp", axis=0, tiled=True),
        lax.all_gather(key_matrix, "dp", axis=0, tiled=True),
        lax.all_gather(value_matrix, "dp", axis=0, tiled=True),
    )
    query, key_rows, raw_values = tuple(
        (jnp.dot(inputs, piece, preferred_element_type=jnp.float32) for piece in pieces)
    )
    value_rows = raw_values.astype(jnp.bfloat16)
    query_norm = rotary_then_norm(query, token_places, QUERY_HEADS)
    key_norm = rotary_then_norm(key_rows, token_places, KEY_VALUE_HEADS)
    kplace = jnp.where(live, token_places + 1, 0)
    head_group = QUERY_HEADS // KEY_VALUE_HEADS
    per_head_queries = query_norm.reshape(token_slots, KEY_VALUE_HEADS, head_group, HEAD_SIZE)

    def add_keys(piece):
        key_portion, value_portion, kpos, kseg = piece
        token_count = key_portion.shape[0]
        kchunk = (kpos - 1 + STRETCH - cstart) // STRETCH
        scores = jnp.einsum(
            "qhgd,khd->hgqk",
            per_head_queries,
            key_portion.reshape(token_count, KEY_VALUE_HEADS, HEAD_SIZE),
            preferred_element_type=jnp.float32,
        ) * (1.0 / math.sqrt(HEAD_SIZE))
        allowed = (kseg[None, :] == qseg[:, None]) & (kchunk[None, :] == qchunk[:, None])
        allowed = allowed & (kpos[None, :] >= 1) & (kpos[None, :] <= token_places[:, None] + 1)
        weights = jnp.where(allowed[None, None], jnp.exp(scores), 0.0)
        denom = jnp.sum(weights, axis=-1)
        numer = jnp.einsum(
            "hgqk,khd->qhgd",
            weights.astype(jnp.bfloat16),
            value_portion.reshape(token_count, KEY_VALUE_HEADS, HEAD_SIZE),
            preferred_element_type=jnp.float32,
        )
        return (numer, denom)

    empty = (
        jnp.zeros((token_slots, KEY_VALUE_HEADS, head_group, HEAD_SIZE), jnp.float32),
        jnp.zeros((KEY_VALUE_HEADS, head_group, token_slots), jnp.float32),
    )
    own_block = (key_norm, value_rows, kplace, qseg)
    piece = (
        lax.all_gather(own_block[0], "ctx", axis=0, tiled=True),
        lax.all_gather(own_block[1], "ctx", axis=0, tiled=True),
        lax.all_gather(own_block[2], "ctx", axis=0, tiled=True),
        lax.all_gather(own_block[3], "ctx", axis=0, tiled=True),
    )
    owner = jnp.int32(0) // token_slots
    numer, denom = lax.cond(
        owner <= mine, lambda state: add_keys(piece), lambda state: state, empty
    )
    denom_rows = jnp.transpose(denom, (2, 0, 1))
    safe = jnp.where(live[:, None, None], denom_rows, 1.0)
    result = numer / safe[..., None] * live[:, None, None, None].astype(jnp.float32)
    attention = result.reshape(token_slots, QUERY_HEADS * HEAD_SIZE).astype(jnp.bfloat16)
    verdict = jnp.dot(attention, score_vector, preferred_element_type=jnp.float32)
    loglik = jax.nn.log_sigmoid(verdict)
    onehot = span_ids[0][:, None] == jnp.arange(CAND, dtype=jnp.int32)[None, :]
    sums = jnp.sum(jnp.where(onehot, loglik[:, None], 0.0), axis=0)
    tally = jnp.sum(onehot.astype(jnp.float32), axis=0)
    sums, tally = lax.psum((sums, tally), "ctx")
    return (attention[None], (sums / tally)[None])


def solution(mesh):
    placed = (
        P("dp", "ctx", None),
        P("dp", None),
        P("dp"),
        P("dp", "ctx"),
        P("dp", "ctx"),
        P("dp", None),
        P("dp", None),
        P("dp", None),
        P(),
    )
    return jax.shard_map(
        per_device,
        mesh=mesh,
        in_specs=placed,
        out_specs=(P("dp", "ctx", None), P("dp", None)),
        check_vma=False,
    )
```

profile of v0, /device:TPU:8, one launch (start us, length us, event | category | flops | bytes accessed | tf_op | source)
XLA Modules:
  0.0 375.7 jit_solution(2490414776641406215)
XLA Ops:
  7.2 0.7 all-gather.8.cloned.1.call-update
  7.9 0.0 all-gather.14.cloned.1.call-start
  8.0 0.7 all-gather.14.cloned.1.call-update
  8.7 0.0 all-gather.12.cloned.1.call-start
  8.7 0.7 all-gather.12.cloned.1.call-update
  9.4 0.0 all-gather.10.cloned.1.call-start
  9.5 1.3 fusion.27
  10.8 0.5 fusion.30
  11.3 0.2 multiply_cosine_fusion
  11.5 38.2 %all-gather.8.cloned.1.call-done = bf16[2560,512]{1,0:T(8,128)(2,1)} async-done(((bf16[160,512]{1,0:T(8,128)(2,1)}), bf16[2560,512]{1,0:T(8,128)(2,1)}) %all-gather.8.cloned.1.call-update) | async-done | bytes 2621456 | tf_op jit(solution)/shard_map/all_gather | solution.py:60
  49.8 3.0 copy.43
  52.8 0.8 fusion.24
  53.8 0.8 copy.44
  54.6 0.0 all-gather.16.cloned.1.call-start
  54.6 34.2 %all-gather.14.cloned.1.call-done = bf16[2560,512]{1,0:T(8,128)(2,1)} async-done(((bf16[160,512]{1,0:T(8,128)(2,1)}), bf16[2560,512]{1,0:T(8,128)(2,1)}) %all-gather.14.cloned.1.call-update) | async-done | bytes 2621456 | tf_op jit(solution)/shard_map/all_gather | solution.py:61
  88.8 2.9 convolution_convert_fusion
  91.7 0.6 reshape.251
  92.4 43.5 %all-gather = s32[1,2048]{1,0:T(1,128)S(1)} all-gather(s32[1,128]{1,0:T(1,128)S(1)} %copy-done.5), channel_id=2, replica_groups=mesh['dp'=16,'ctx'=16] {'ctx'}, dimensions={1}, use_global_device_ids=true | all-gather | bytes 8704 | tf_op jit(solution)/shard_map/all_gather | solution.py:104
  135.8 1.2 select_bitcast_fusion.1
  137.0 38.0 %all-gather.1 = s32[16,1,128]{2,1,0:T(1,128)S(1)} all-gather(s32[1,1,128]{2,1,0:T(1,128)S(1)} %select_bitcast_fusion.1), channel_id=1, replica_groups=mesh['dp'=16,'ctx'=16] {'ctx'}, dimensions={0}, use_global_device_ids=true | all-gather | bytes 8704 | tf_op jit(solution)/shard_map/all_gather | solution.py:103
  175.0 0.5 iota_add_fusion
  175.5 1.2 fusion.31
  176.7 1.2 iota_compare_fusion.1
  177.9 17.7 %copy.45 = bf16[2560,2560]{1,0:T(8,128)(2,1)} copy(bf16[2560,2560]{0,1:T(8,128)(2,1)} %bitcast.64) | data formatting | bytes 26214400 | tf_op jit(solution)/shard_map/dot_general | solution.py:64
  195.6 6.6 %fusion.22 = f32[128,20,128]{0,2,1:T(8,128)S(1)} fusion(bf16[20,128,2560]{2,1,0:T(8,128)(2,1)} %bitcast.63, bf16[1,128,2560]{2,1,0:T(8,128)(2,1)S(1)} %copy-done), kind=kOutput, calls=%fused_computation.37 | convolution fusion | flops 1677721600 | bytes 15073280 | tf_op jit(solution)/shard_map/dot_general | solution.py:64
  202.2 0.2 multiply_subtract_fusion
  202.4 0.4 copy.47
  202.8 1.5 copy.46
  204.3 0.1 fusion.20
  204.4 2.1 fusion.19
  206.5 24.0 %all-gather.10.cloned.1.call-done = bf16[2048,512]{1,0:T(8,128)(2,1)} async-done(((bf16[128,512]{1,0:T(8,128)(2,1)}), bf16[2048,512]{1,0:T(8,128)(2,1)}) %all-gather.10.cloned.1.call-update) | async-done | bytes 2097168 | tf_op jit(solution)/shard_map/all_gather | solution.py:101
  230.5 59.5 %all-gather.16.cloned.1.call-done = bf16[2048,512]{1,0:T(8,128)(2,1)} async-done(((bf16[128,512]{1,0:T(8,128)(2,1)}), bf16[2048,512]{1,0:T(8,128)(2,1)}) %all-gather.16.cloned.1.call-update) | async-done | bytes 2097168 | tf_op jit(solution)/shard_map/all_gather | solution.py:102
  290.0 32.8 %conditional.1 = (f32[4,5,128]{2,1,0:T(8,128)}, f32[128,4,5,128]{0,3,2,1:T(8,128)S(1)}) conditional(s32[]{:T(128)} %convert_element_type.59, () %tuple.28, (s32[2048]{0:T(1024)S(1)}, s32[1,128]{1,0:T(1,128)S(1)}, s32[2048]{0:T(1024)S(1)}, s32[]{:T(128)}, s32[128]{0:T(128)S(1)}, /*index=5*/s32[128]{0:T(128)S(1)}, s32[]{:T(128)}, s32[]{:T(128)}, ...), branch_computations={%region_4.5_spmd, %region_5.7_spmd.clone.clone} | conditional | flops 2717421312 | bytes 68356152 | solution.py:107
  290.0 0.7 and_select_fusion
  290.7 0.7 add_select_fusion
  291.4 1.9 compare_and_fusion
  293.3 4.0 %reshape.253 = bf16[2048,4,128]{2,1,0:T(4,128)(2,1)} reshape(bf16[2048,512]{1,0:T(8,128)(2,1)} %get-tuple-element.241) | data formatting | bytes 4194304 | tf_op jit(solution)/shard_map/cond/branch_1_fun/reshape | solution.py:80
  297.3 11.2 %fusion = (f32[4,5,128]{2,1,0:T(8,128)}, f32[4,2048,128,5]{2,1,3,0:T(8,128)}) fusion(pred[128,2048]{0,1:T(8,128)(4,1)S(1)} %compare_and_fusion, bf16[128,4,5,128]{3,0,2,1:T(8,128)(2,1)S(1)} %get-tuple-element.242, bf16[2048,4,128,1]{2,1,0,3:T(4,128)(2,1)} %bitcast.72), kind=kOutput, calls=%fused_computation.1 | convolution fusion | flops 1357903360 | bytes 23996416 | tf_op jit(solution)/shard_map/cond/branch_1_fun/qhgd,khd->hgqk/dot_general | solution.py:77
  308.5 2.1 reshape.254
  310.6 11.9 %fusion.10 = f32[128,4,5,128]{3,0,2,1:T(8,128)S(1)} fusion(bf16[2048,4,128,1]{2,1,0,3:T(4,128)(2,1)} %bitcast.71, f32[4,2048,128,5]{2,1,3,0:T(8,128)} %get-tuple-element.266, pred[128,2048]{0,1:T(8,128)(4,1)S(1)} %compare_and_fusion), kind=kOutput, calls=%fused_computation.10 | convolution fusion | flops 1357905920 | bytes 24641536 | tf_op jit(solution)/shard_map/cond/branch_1_fun/hgqk,khd->qhgd/dot_general | solution.py:87
  322.4 0.4 copy.61
  322.9 0.8 select_bitcast_fusion
  323.7 0.9 multiply_convert_fusion
  324.5 1.1 copy.49
  325.6 0.2 fusion.29
  325.8 0.1 convert_reduce_fusion
  326.0 42.6 %all-reduce = (f32[32]{0:T(128)S(1)}, f32[32]{0:T(128)S(1)}) all-reduce(f32[32]{0:T(128)S(1)} %get-tuple-element.260, f32[32]{0:T(128)S(1)} %get-tuple-element.259), channel_id=1, replica_groups=mesh['dp'=16,'ctx'=16] {'ctx'}, use_global_device_ids=true, to_apply=%region_8.9 | all-reduce | flops 64 | bytes 512 | tf_op jit(solution)/shard_map/psum | solution.py:119
  368.6 0.5 divide_bitcast_fusion
  (27 shorter events, 0.2 us)
Async XLA Ops:
  7.2 45.6 %copy-start = (bf16[1,128,2560]{2,1,0:T(8,128)(2,1)S(1)}, bf16[1,128,2560]{2,1,0:T(8,128)(2,1)}, u32[]{:S(2)}) copy-start(bf16[1,128,2560]{2,1,0:T(8,128)(2,1)} %param.11) | copy-start | bytes 1966084
  7.2 42.6 %all-gather.8.cloned.1.call-start = ((), (), s32[]{:S(2)}) async-start(), calls=%async_computation | async-start | bytes 2785280 | tf_op jit(solution)/shard_map/all_gather | solution.py:60
  7.9 80.9 %all-gather.14.cloned.1.call-start = ((), (), s32[]{:S(2)}) async-start(), calls=%async_computation.3 | async-start | bytes 2785280 | tf_op jit(solution)/shard_map/all_gather | solution.py:61
  8.7 169.2 %all-gather.12.cloned.1.call-start = ((), (), s32[]{:S(2)}) async-start(), calls=%async_computation.2 | async-start | bytes 13926400 | tf_op jit(solution)/shard_map/all_gather | solution.py:59
  9.4 221.1 %all-gather.10.cloned.1.call-start = ((), (), s32[]{:S(2)}) async-start(), calls=%async_computation.1 | async-start | bytes 2228224 | tf_op jit(solution)/shard_map/all_gather | solution.py:101
  53.7 38.0 %copy-start.4 = (bf16[2560]{0:T(1024)(128)(2,1)S(1)}, bf16[2560]{0:T(1024)(128)(2,1)}, u32[]{:S(2)}) copy-start(bf16[2560]{0:T(1024)(128)(2,1)} %param.19) | copy-start | bytes 15364
  53.7 38.6 %copy-start.5 = (s32[1,128]{1,0:T(1,128)S(1)}, s32[1,128]{1,0:T(1,128)}, u32[]{:S(2)}) copy-start(s32[1,128]{1,0:T(1,128)} %param.14) | copy-start | bytes 1540
  54.6 235.5 %all-gather.16.cloned.1.call-start = ((), (), s32[]{:S(2)}) async-start(), calls=%async_computation.4 | async-start | bytes 2228224 | tf_op jit(solution)/shard_map/all_gather | solution.py:102
  297.3 11.2 %copy-start.2 = (bf16[2048,512]{1,0:T(8,128)(2,1)S(1)}, bf16[2048,512]{1,0:T(8,128)(2,1)}, u32[]{:S(2)}) copy-start(bf16[2048,512]{1,0:T(8,128)(2,1)} %get-tuple-element.243) | copy-start | bytes 6291460 | tf_op jit(solution)/shard_map/cond
  322.8 2.8 copy-start.3
  322.9 3.0 copy-start.6
  322.9 46.3 %copy-start.1 = (bf16[1,128,2560]{2,1,0:T(8,128)(2,1)S(1)}, bf16[1,128,2560]{2,1,0:T(8,128)(2,1)}, u32[]{:S(2)}) copy-start(bf16[1,128,2560]{2,1,0:T(8,128)(2,1)} %param.11) | copy-start | bytes 1966084
Sparse Core Ops, SparseCore 0:
  9.8 39.9 all-gather.7
  51.6 37.1 all-gather.13
  90.7 76.7 all-gather.11
  170.3 60.1 all-gather.9
  232.8 57.2 all-gather.15
where the time goes:
time: 376 us
  waiting for transfers between devices  158 us (42%)
  blocking collectives  124 us (33%)
  matrix products  33.7 us (9%)
  local copies, waits for them, and re-layouts  31.5 us (8%)
  other arithmetic  14.1 us (4%)
  between operations  14 us (4%)
    all_gather x1, waiting for transfers between devices, per_device(): lax.all_gather(own_block[1], 'ctx', axis=0, tiled=True)  59.5 us
    all_gather x1, blocking collectives, per_device(): lax.all_gather(own_block[3], 'ctx', axis=0, tiled=True)  43.5 us
    psum x1, blocking collectives, per_device(): sums, tally = lax.psum((sums, tally), 'ctx')  42.6 us
    all_gather x1, waiting for transfers between devices, per_device(): lax.all_gather(key_matrix, 'dp', axis=0, tiled=True)  38.2 us
    all_gather x1, blocking collectives, per_device(): lax.all_gather(own_block[2], 'ctx', axis=0, tiled=True)  38 us
    all_gather x1, waiting for transfers between devices, per_device(): lax.all_gather(value_matrix, 'dp', axis=0, tiled=True)  34.2 us
    all_gather x1, waiting for transfers between devices, per_device(): lax.all_gather(own_block[0], 'ctx', axis=0, tiled=True)  24 us
    dot_general x2, local copies, waits for them, and re-layouts, per_device(): jnp.dot(inputs, piece, preferred_element_type=jnp.float32)  20.7 us
  transfers between devices with their start and end apart: 5, of which 4 were waited for; matrix products, arithmetic and copies ran while one was open for 11% of the time, Pallas kernels for 0%

commit v1 on v0

--- a/solution.py
+++ b/solution.py
@@ -1,3 +1,4 @@
+import functools
 import math
 import jax
 import jax.numpy as jnp
@@ -11,6 +12,16 @@
 CAND = 32
 THETA = 500000.0
 EPS = 1e-05
+
+
+def tell_wires_up(base_x, axis_key):
+    g_now = lax.psum(1, axis_key)
+    n_now = jnp.stack([base_x] * g_now)
+    moved = lax.all_to_all(n_now, axis_key, 0, 0)
+    return jnp.concatenate(moved, 0)
+
+
+switch_rows = functools.partial(tell_wires_up, axis_key="dp")
 
 
 def rotary_then_norm(value_rows, token_places, heads):
@@ -58,7 +69,7 @@
     pieces = (
         lax.all_gather(query_weight, "dp", axis=0, tiled=True),
         lax.all_gather(key_matrix, "dp", axis=0, tiled=True),
-        lax.all_gather(value_matrix, "dp", axis=0, tiled=True),
+        switch_rows(value_matrix),
     )
     query, key_rows, raw_values = tuple(
         (jnp.dot(inputs, piece, preferred_element_type=jnp.float32) for piece in pieces)

time: 376 us -> 356 us (0.947)
  waiting for transfers between devices: 158 us -> 130 us
  starting transfers between devices: 0.19 us -> 6.57 us
  local copies, waits for them, and re-layouts: 31.5 us -> 36.2 us
    all_gather x1 -> x0, waiting for transfers between devices: 34.2 us -> none  [per_device(): lax.all_gather(value_matrix, 'dp', axis=0, tiled=True)]
    all_gather x1, waiting for transfers between devices: 38.2 us -> 49 us  [per_device(): lax.all_gather(key_matrix, 'dp', axis=0, tiled=True)]
    all_to_all x0 -> x1, starting transfers between devices: none -> 6.42 us  [tell_wires_up(): moved = lax.all_to_all(n_now, axis_key, 0, 0)]
    all_gather x1, waiting for transfers between devices: 24 us -> 19.8 us  [per_device(): lax.all_gather(own_block[0], 'ctx', axis=0, tiled=True)]
  transfers between devices with their start and end apart: 5 -> 5, of which waited for: 4 -> 3; matrix products, arithmetic and copies ran while one was open for 11% -> 13% of each run, Pallas kernels for 0% -> 0%
where the time goes in v1:
time: 356 us; the launch traced here: 355 us
  waiting for transfers between devices  130 us (37%)
  blocking collectives  125 us (35%)
  local copies, waits for them, and re-layouts  36.2 us (10%)
  matrix products  32.5 us (9%)
  between operations  14 us (4%)
  other arithmetic  11.2 us (3%)
  starting transfers between devices  6.57 us (2%)
    all_gather x1, waiting for transfers between devices, per_device(): lax.all_gather(own_block[1], 'ctx', axis=0, tiled=True)  59.6 us
    all_gather x1, waiting for transfers between devices, per_device(): lax.all_gather(key_matrix, 'dp', axis=0, tiled=True)  49 us
    all_gather x1, blocking collectives, per_device(): lax.all_gather(own_block[3], 'ctx', axis=0, tiled=True)  44.4 us
    psum x1, blocking collectives, per_device(): sums, tally = lax.psum((sums, tally), 'ctx')  42.7 us
    all_gather x1, blocking collectives, per_device(): lax.all_gather(own_block[2], 'ctx', axis=0, tiled=True)  38 us
    dot_general x2, local copies, waits for them, and re-layouts, per_device(): jnp.dot(inputs, piece, preferred_element_type=jnp.float32)  22 us
    all_gather x1, waiting for transfers between devices, per_device(): lax.all_gather(own_block[0], 'ctx', axis=0, tiled=True)  19.8 us
    dot_general x1, matrix products, add_keys(): jnp.einsum('hgqk,khd->qhgd', weights.astype(jnp.bfloat16), value_portion....  11.3 us
  transfers between devices with their start and end apart: 5, of which 3 were waited for; matrix products, arithmetic and copies ran while one was open for 13% of the time, Pallas kernels for 0%

profile of v1, /device:TPU:8, one launch (start us, length us, event | category | flops | bytes accessed | tf_op | source)
XLA Modules:
  0.0 355.3 jit_solution(7670964878780520455)
XLA Ops:
  7.2 0.0 all-gather.7.cloned.1.call-start
  7.2 0.7 all-gather.7.cloned.1.call-update
  7.9 0.0 all-gather.11.cloned.1.call-start
  8.0 0.7 all-gather.11.cloned.1.call-update
  8.7 2.6 stack.2
  11.3 6.4 %all-to-all-start = ((bf16[16,160,512]{2,1,0:T(8,128)(2,1)}), bf16[16,160,512]{2,1,0:T(8,128)(2,1)S(1)}, u32[]{:S(2)}, u32[]{:S(2)}) async-start(bf16[16,160,512]{2,1,0:T(8,128)(2,1)} %stack.2), calls=%async_computation | async-start | bytes 5242880 | tf_op jit(solution)/shard_map/all_to_all | solution.py:20
  17.7 0.0 all-gather.9.cloned.1.call-start
  17.8 0.7 fusion.27
  18.5 0.6 fusion.30
  19.1 0.2 multiply_cosine_fusion
  19.3 49.0 %all-gather.7.cloned.1.call-done = bf16[2560,512]{1,0:T(8,128)(2,1)} async-done(((bf16[160,512]{1,0:T(8,128)(2,1)}), bf16[2560,512]{1,0:T(8,128)(2,1)}) %all-gather.7.cloned.1.call-update) | async-done | bytes 2621456 | tf_op jit(solution)/shard_map/all_gather | solution.py:71
  68.3 4.4 %copy.43 = bf16[512,2560]{1,0:T(8,128)(2,1)} copy(bf16[512,2560]{0,1:T(8,128)(2,1)} %bitcast.72) | data formatting | bytes 5242880 | tf_op jit(solution)/shard_map/dot_general | solution.py:75
  72.7 2.6 fusion.24
  75.4 0.8 copy.44
  76.2 0.0 all-gather.9.cloned.1.call-update
  76.2 0.0 all-gather.13.cloned.1.call-start
  76.3 1.2 convolution_convert_fusion
  77.5 44.4 %all-gather = s32[1,2048]{1,0:T(1,128)S(1)} all-gather(s32[1,128]{1,0:T(1,128)S(1)} %copy-done.4), channel_id=2, replica_groups=mesh['dp'=16,'ctx'=16] {'ctx'}, dimensions={1}, use_global_device_ids=true | all-gather | bytes 8704 | tf_op jit(solution)/shard_map/all_gather | solution.py:115
  121.9 1.2 select_bitcast_fusion.1
  123.1 38.0 %all-gather.1 = s32[16,1,128]{2,1,0:T(1,128)S(1)} all-gather(s32[1,1,128]{2,1,0:T(1,128)S(1)} %select_bitcast_fusion.1), channel_id=1, replica_groups=mesh['dp'=16,'ctx'=16] {'ctx'}, dimensions={0}, use_global_device_ids=true | all-gather | bytes 8704 | tf_op jit(solution)/shard_map/all_gather | solution.py:114
  161.1 0.6 iota_add_fusion
  161.8 0.6 fusion.31
  162.4 0.6 iota_compare_fusion.1
  163.0 0.0 all-gather.11.cloned.1.call-done
  163.0 17.6 %copy.45 = bf16[2560,2560]{1,0:T(8,128)(2,1)} copy(bf16[2560,2560]{0,1:T(8,128)(2,1)} %bitcast.65) | data formatting | bytes 26214400 | tf_op jit(solution)/shard_map/dot_general | solution.py:75
  180.7 6.6 %fusion.22 = f32[128,20,128]{0,2,1:T(8,128)S(1)} fusion(bf16[20,128,2560]{2,1,0:T(8,128)(2,1)} %bitcast.64, bf16[1,128,2560]{2,1,0:T(8,128)(2,1)S(1)} %copy-done), kind=kOutput, calls=%fused_computation.37 | convolution fusion | flops 1677721600 | bytes 15073280 | tf_op jit(solution)/shard_map/dot_general | solution.py:75
  187.3 0.2 multiply_subtract_fusion
  187.5 0.4 copy.47
  187.9 1.5 copy.46
  189.4 0.1 fusion.20
  189.5 2.1 fusion.19
  191.6 19.8 %all-gather.9.cloned.1.call-done = bf16[2048,512]{1,0:T(8,128)(2,1)} async-done(((bf16[128,512]{1,0:T(8,128)(2,1)}), bf16[2048,512]{1,0:T(8,128)(2,1)}) %all-gather.9.cloned.1.call-update) | async-done | bytes 2097168 | tf_op jit(solution)/shard_map/all_gather | solution.py:112
  211.4 59.6 %all-gather.13.cloned.1.call-done = bf16[2048,512]{1,0:T(8,128)(2,1)} async-done(((bf16[128,512]{1,0:T(8,128)(2,1)}), bf16[2048,512]{1,0:T(8,128)(2,1)}) %all-gather.13.cloned.1.call-update) | async-done | bytes 2097168 | tf_op jit(solution)/shard_map/all_gather | solution.py:113
  271.0 32.9 %conditional.1 = (f32[4,5,128]{2,1,0:T(8,128)S(1)}, f32[128,4,5,128]{0,3,2,1:T(8,128)S(1)}) conditional(s32[]{:T(128)} %convert_element_type.59, () %tuple.28, (s32[2048]{0:T(1024)S(1)}, s32[1,128]{1,0:T(1,128)S(1)}, s32[2048]{0:T(1024)S(1)}, s32[]{:T(128)}, s32[128]{0:T(128)S(1)}, /*index=5*/s32[128]{0:T(128)S(1)}, s32[]{:T(128)}, ...), branch_computations={%region_4.5_spmd, %region_5.7_spmd.clone.clone} | conditional | flops 2717421312 | bytes 68356152 | solution.py:118
  271.0 0.7 and_select_fusion
  271.6 0.7 add_select_fusion
  272.3 1.9 compare_and_fusion
  274.2 4.0 %reshape.259 = bf16[2048,4,128]{2,1,0:T(4,128)(2,1)} reshape(bf16[2048,512]{1,0:T(8,128)(2,1)} %get-tuple-element.241) | data formatting | bytes 4194304 | tf_op jit(solution)/shard_map/cond/branch_1_fun/reshape | solution.py:91
  278.2 10.6 %fusion = (f32[4,5,128]{2,1,0:T(8,128)S(1)}, f32[4,2048,128,5]{2,1,3,0:T(8,128)}) fusion(pred[128,2048]{0,1:T(8,128)(4,1)S(1)} %compare_and_fusion, bf16[128,4,5,128]{3,0,2,1:T(8,128)(2,1)S(1)} %get-tuple-element.242, bf16[2048,4,128,1]{2,1,0,3:T(4,128)(2,1)} %bitcast.74), kind=kOutput, calls=%fused_computation.1 | convolution fusion | flops 1357903360 | bytes 23996416 | tf_op jit(solution)/shard_map/cond/branch_1_fun/qhgd,khd->hgqk/dot_general | solution.py:88
  288.9 2.1 reshape.260
  290.9 11.3 %fusion.10 = f32[128,4,5,128]{3,0,2,1:T(8,128)} fusion(bf16[2048,4,128,1]{2,1,0,3:T(4,128)(2,1)} %bitcast.73, f32[4,2048,128,5]{2,1,3,0:T(8,128)} %get-tuple-element.266, pred[128,2048]{0,1:T(8,128)(4,1)S(1)} %compare_and_fusion), kind=kOutput, calls=%fused_computation.10 | convolution fusion | flops 1357905920 | bytes 24641536 | tf_op jit(solution)/shard_map/cond/branch_1_fun/hgqk,khd->qhgd/dot_general | solution.py:98
  302.2 1.7 copy.61
  303.9 0.2 multiply_convert_fusion
  304.1 1.1 copy.49
  305.2 0.2 fusion.29
  305.4 0.1 convert_reduce_fusion
  305.5 42.7 %all-reduce = (f32[32]{0:T(128)S(1)}, f32[32]{0:T(128)S(1)}) all-reduce(f32[32]{0:T(128)S(1)} %get-tuple-element.260, f32[32]{0:T(128)S(1)} %get-tuple-element.259), channel_id=1, replica_groups=mesh['dp'=16,'ctx'=16] {'ctx'}, use_global_device_ids=true, to_apply=%region_8.9 | all-reduce | flops 64 | bytes 512 | tf_op jit(solution)/shard_map/psum | solution.py:130
  348.2 0.5 divide_bitcast_fusion
  (27 shorter events, 0.2 us)
Async XLA Ops:
  7.2 65.6 %copy-start = (bf16[1,128,2560]{2,1,0:T(8,128)(2,1)S(1)}, bf16[1,128,2560]{2,1,0:T(8,128)(2,1)}, u32[]{:S(2)}) copy-start(bf16[1,128,2560]{2,1,0:T(8,128)(2,1)} %param.11) | copy-start | bytes 1966084
  7.2 61.2 %all-gather.7.cloned.1.call-start = ((), (), s32[]{:S(2)}) async-start(), calls=%async_computation.1 | async-start | bytes 2785280 | tf_op jit(solution)/shard_map/all_gather | solution.py:71
  7.9 155.1 %all-gather.11.cloned.1.call-start = ((), (), s32[]{:S(2)}) async-start(), calls=%async_computation.3 | async-start | bytes 13926400 | tf_op jit(solution)/shard_map/all_gather | solution.py:70
  11.3 6.5 %copy-start.5 = (s32[1,16]{1,0:T(1,128)S(1)}, s32[1,16]{1,0:T(1,128)}, u32[]{:S(2)}) copy-start(s32[1,16]{1,0:T(1,128)} %param.12) | copy-start | bytes 196
  11.3 65.0 %all-to-all-start = ((bf16[16,160,512]{2,1,0:T(8,128)(2,1)}), bf16[16,160,512]{2,1,0:T(8,128)(2,1)S(1)}, u32[]{:S(2)}, u32[]{:S(2)}) async-start(bf16[16,160,512]{2,1,0:T(8,128)(2,1)} %stack.2), calls=%async_computation | async-start | bytes 5242880 | tf_op jit(solution)/shard_map/all_to_all | solution.py:20
  17.7 193.7 %all-gather.9.cloned.1.call-start = ((), (), s32[]{:S(2)}) async-start(), calls=%async_computation.2 | async-start | bytes 2228224 | tf_op jit(solution)/shard_map/all_gather | solution.py:112
  75.4 2.1 copy-start.3
  75.4 2.1 copy-start.4
  76.2 194.7 %all-gather.13.cloned.1.call-start = ((), (), s32[]{:S(2)}) async-start(), calls=%async_computation.4 | async-start | bytes 2228224 | tf_op jit(solution)/shard_map/all_gather | solution.py:113
  278.2 10.7 %copy-start.2 = (bf16[2048,512]{1,0:T(8,128)(2,1)S(1)}, bf16[2048,512]{1,0:T(8,128)(2,1)}, u32[]{:S(2)}) copy-start(bf16[2048,512]{1,0:T(8,128)(2,1)} %get-tuple-element.243) | copy-start | bytes 6291460 | tf_op jit(solution)/shard_map/cond
  303.9 1.5 copy-start.6
  303.9 44.8 %copy-start.1 = (bf16[1,128,2560]{2,1,0:T(8,128)(2,1)S(1)}, bf16[1,128,2560]{2,1,0:T(8,128)(2,1)}, u32[]{:S(2)}) copy-start(bf16[1,128,2560]{2,1,0:T(8,128)(2,1)} %param.11) | copy-start | bytes 1966084
Sparse Core Ops, SparseCore 0:
  9.8 58.4 all-gather.6
  70.2 78.0 all-gather.10
  151.3 60.1 all-gather.8
  213.7 57.2 all-gather.12
